TPU v7x, 32 devices: a whole 2x2x4 slice. The times are simulated.
32 devices in a mesh: sum: 8 (over z, x), mode: 4 (over y, core).
Axes of the slice: x: 2, y: 2, z: 4, core: 2. Of those that a mesh axis runs over, the one named last changes fastest.
Arguments:
- left_cores: bfloat16 [8, 512, 64, 512], P('sum', None, 'mode'), may hold values from -80 to 80, as said below
- right_cores: bfloat16 [8, 512, 64, 512], P('sum', None, 'mode'), may hold values from -6 to 6
- sketch: bfloat16 [64, 512, 512], P('mode'), may hold values from -0.03125 to 0.03125
Outputs:
- basis_core: float32 [512, 64, 512], P('sum', 'mode')
- carries: float32 [8, 512, 512], P('sum')
Inputs may be any that keep to these rules, and one draw needn't show every extreme that they name: `left_cores`: independent entries; each row (summand, left rank, mode index) has its own scale.
All inputs are finite; a program needn't handle non-finite values.
Results may differ from a plain program's by a relative error of at most 0.0035.
Values may be sent and summed in bfloat16 or wider, within the bound.
No kernel may reach another device: no remote copies, remote signals or barrier semaphores. Data moves between devices by JAX's collectives and lax.ppermute only.
A program may use at most 128 MiB of HBM per device.

v0:
```python
import math
import jax
import jax.numpy as jnp
from jax import lax
from jax.experimental.layout import Layout, with_layout_constraint
from jax.sharding import PartitionSpec as P

R_IN = 512
MODES = 64
BLOCK = 128
HI = lax.Precision.HIGHEST


def mm(a, b):
    return jnp.dot(a, b, precision=HI, preferred_element_type=jnp.float32)


def orthonormal(sketched, gram):
    n = gram.shape[0]
    b = min(BLOCK, n)
    nb = n // b
    eye = jnp.eye(b, dtype=jnp.float32)
    inverses = []
    panels = []
    trailing = gram
    for k in range(nb):
        diag = trailing[:b, :b]
        lkk = jnp.linalg.cholesky(diag)
        ikk = lax.linalg.triangular_solve(lkk, eye, left_side=True, lower=True)
        inverses.append(ikk)
        if k < nb - 1:
            panel = mm(trailing[b:, :b], ikk.T)
            panels.append(panel)
            trailing = trailing[b:, b:] - mm(panel, panel.T)
    blocks = []
    for k in range(nb):
        rhs = sketched[:, k * b : (k + 1) * b]
        if k > 0:
            done = jnp.concatenate(blocks, axis=1)
            lrow = jnp.concatenate(
                [panels[j][(k - j - 1) * b : (k - j) * b] for j in range(k)], axis=1
            )
            rhs = rhs - mm(done, lrow.T)
        blocks.append(mm(rhs, inverses[k].T))
    return jnp.concatenate(blocks, axis=1)


def per_device(left_cores, right_cores, sketch):
    sum_local, rows_in, mode_local, rank_width = left_cores.shape
    target = sketch.shape[2]
    partial_map = lax.dot_general(
        right_cores, sketch, (((2, 3), (0, 1)), ((), ())), preferred_element_type=jnp.float32
    )
    mapped = lax.psum(partial_map, "mode").astype(jnp.bfloat16)
    local_sum = lax.dot_general(
        left_cores, mapped, (((0, 3), (0, 1)), ((), ())), preferred_element_type=jnp.float32
    )
    local_sum = with_layout_constraint(local_sum, Layout(major_to_minor=(0, 1, 2)))
    factor = math.sqrt(R_IN * MODES)
    share = lax.psum_scatter(local_sum, "sum", scatter_dimension=0, tiled=True)
    flat_share = share.reshape(-1, target)
    gram_part = jnp.dot(flat_share.T, flat_share, precision=HI)
    gram = lax.psum(gram_part, ("sum", "mode"))
    basis = orthonormal(flat_share, gram)
    block = basis.reshape(share.shape)
    rounded = block.astype(jnp.bfloat16)
    pieces = lax.all_gather(rounded, "sum", axis=0, tiled=True)
    partial_carry = lax.dot_general(
        pieces, left_cores, (((0, 1), (1, 2)), ((), ())), preferred_element_type=jnp.float32
    )
    partial_carry = jnp.transpose(partial_carry, (1, 0, 2))
    carries = lax.psum(partial_carry, "mode")
    return (block * factor, carries)


def solution(mesh):
    in_specs = (P("sum", None, "mode", None), P("sum", None, "mode", None), P("mode", None, None))
    out_specs = (P("sum", "mode", None), P("sum", None, None))
    return jax.shard_map(
        per_device, mesh=mesh, in_specs=in_specs, out_specs=out_specs, check_vma=False
    )
```

profile of v0, /device:TPU:0, one launch (start us, length us, event | category | flops | bytes accessed | tf_op | source)
XLA Modules:
  0.0 789.0 jit_solution(3310593755060591880)
XLA Ops:
  7.2 17.1 %fusion.10 = f32[1,512,512]{2,1,0:T(8,128)S(1)} fusion(bf16[16,512,512]{2,1,0:T(8,128)(2,1)} %param.8, bf16[512,16,512]{2,1,0:T(8,128)(2,1)} %bitcast.84), kind=kOutput, calls=%fused_computation.13 | convolution fusion | flops 4294967296 | bytes 17825792 | tf_op jit(solution)/shard_map/dot_general | solution.py:51
  24.3 28.0 %all-reduce.7 = bf16[1,512,512]{2,1,0:T(8,128)(2,1)S(1)} all-reduce(f32[1,512,512]{2,1,0:T(8,128)S(1)} %fusion.10), channel_id=1, replica_groups=mesh['sum'=8,'mode'=4] {'mode'}, use_global_device_ids=true, to_apply=%region_0.0 | all-reduce | flops 262144 | bytes 1572864 | tf_op jit(solution)/shard_map/psum | solution.py:54
  52.3 11.6 %convolution_bitcast_fusion = f32[512,16,512]{2,1,0:T(8,128)} fusion(bf16[1,512,512]{2,1,0:T(8,128)(2,1)S(1)} %all-reduce.7, bf16[1,512,16,512]{3,2,1,0:T(8,128)(2,1)} %param.6), kind=kOutput, calls=%fused_computation | convolution fusion | flops 4294967296 | bytes 25690112 | tf_op jit(solution)/shard_map/dot_general | solution.py:55
  64.0 0.3 all-reduce.4.cloned.1.call-start
  64.3 282.3 %reduce-scatter.2.cloned.1.call-done = f32[64,16,512]{2,1,0:T(8,128)} async-done(((f32[512,16,512]{2,1,0:T(8,128)}), f32[64,16,512]{2,1,0:T(8,128)}) %reduce-scatter.2.cloned.1.call-update) | async-done | bytes 2097168 | tf_op jit(solution)/shard_map/reduce_scatter | solution.py:60
  346.6 6.7 convolution_bitcast_fusion.1
  353.4 129.0 %all-reduce.4.cloned.1.call-done = f32[512,512]{0,1:T(8,128)} async-done(((f32[512,512]{0,1:T(8,128)}), f32[512,512]{0,1:T(8,128)}) %all-reduce.4.cloned.1.call-update) | async-done | bytes 1048592 | tf_op jit(solution)/shard_map/psum | solution.py:63
  482.4 0.8 slice.79
  483.3 0.9 fusion.62
  484.2 11.7 %cholesky.74 = f32[128,128]{1,0:T(8,128)S(1)} custom-call(f32[128,128]{1,0:T(8,128)S(1)} %fusion.62), custom_call_target="Cholesky" | custom-call | tf_op jit(solution)/shard_map/jit(cholesky)/cholesky | solution.py:28
  495.9 0.6 compare_reduce_fusion.3
  496.6 0.7 fusion.48
  497.2 9.8 %custom-call.8 = f32[1,128,128]{1,2,0:T(8,128)S(1)} custom-call(f32[1,128,128]{2,1,0:T(8,128)S(1)} %fusion.48), custom_call_target="InvertDiagBlocksLowerTriangular" | custom-call | tf_op jit(solution)/shard_map/triangular_solve/custom-call.0 | solution.py:29
  507.4 1.2 fusion.28
  508.6 1.7 convolution_subtract_fusion
  510.5 11.7 %cholesky.85 = f32[128,128]{1,0:T(8,128)S(1)} custom-call(f32[128,128]{1,0:T(8,128)S(1)} %fusion.60), custom_call_target="Cholesky" | custom-call | tf_op jit(solution)/shard_map/jit(cholesky)/cholesky | solution.py:28
  522.2 0.6 compare_reduce_fusion.2
  522.9 0.7 fusion.49
  523.5 18.5 %custom-call.9 = f32[1,128,128]{1,2,0:T(8,128)S(1)} custom-call(f32[1,128,128]{2,1,0:T(8,128)S(1)} %fusion.49), custom_call_target="InvertDiagBlocksLowerTriangular" | custom-call | tf_op jit(solution)/shard_map/triangular_solve/custom-call.0 | solution.py:29
  542.6 0.4 convolution_subtract_fusion.3
  543.1 0.7 fusion.66
  543.9 11.7 %cholesky.96 = f32[128,128]{1,0:T(8,128)S(1)} custom-call(f32[128,128]{1,0:T(8,128)S(1)} %fusion.58), custom_call_target="Cholesky" | custom-call | tf_op jit(solution)/shard_map/jit(cholesky)/cholesky | solution.py:28
  555.6 0.7 compare_reduce_fusion.1
  556.3 0.6 fusion.50
  556.9 9.8 %custom-call.10 = f32[1,128,128]{1,2,0:T(8,128)S(1)} custom-call(f32[1,128,128]{2,1,0:T(8,128)S(1)} %fusion.50), custom_call_target="InvertDiagBlocksLowerTriangular" | custom-call | tf_op jit(solution)/shard_map/triangular_solve/custom-call.0 | solution.py:29
  566.7 0.3 fusion.37
  567.2 0.3 convolution_subtract_fusion.4
  567.6 11.9 %cholesky.107 = f32[128,128]{1,0:T(8,128)S(1)} custom-call(f32[128,128]{1,0:T(8,128)S(1)} %fusion.56), custom_call_target="Cholesky" | custom-call | tf_op jit(solution)/shard_map/jit(cholesky)/cholesky | solution.py:28
  579.6 0.7 compare_reduce_fusion
  580.2 0.6 fusion.51
  580.9 9.8 %custom-call.11 = f32[1,128,128]{1,2,0:T(8,128)S(1)} custom-call(f32[1,128,128]{2,1,0:T(8,128)S(1)} %fusion.51), custom_call_target="InvertDiagBlocksLowerTriangular" | custom-call | tf_op jit(solution)/shard_map/triangular_solve/custom-call.0 | solution.py:29
  591.0 0.6 fusion.24
  591.6 1.0 convolution_subtract_fusion.2
  592.6 0.6 fusion.68
  593.3 2.7 convolution_subtract_fusion.1
  595.9 0.6 fusion.69
  596.6 2.8 fusion.16
  599.4 0.6 fusion.70
  600.0 0.8 copy-done.2
  601.0 0.5 copy.35
  601.5 1.5 copy.36
  603.1 0.3 all-reduce.6.cloned.1.call-start
  603.4 123.7 %all-gather.2.cloned.1.call-done = bf16[512,16,512]{2,0,1:T(8,128)(2,1)} async-done(((bf16[64,16,512]{2,0,1:T(8,128)(2,1)}), bf16[512,16,512]{2,0,1:T(8,128)(2,1)}) %all-gather.2.cloned.1.call-update) | async-done | bytes 8388624 | tf_op jit(solution)/shard_map/all_gather | solution.py:67
  727.1 18.2 %fusion.13 = f32[1,512,512]{2,1,0:T(8,128)} fusion(bf16[512,16,512]{2,0,1:T(8,128)(2,1)} %all-gather.2.cloned.1.call-done, bf16[512,16,512]{2,1,0:T(8,128)(2,1)} %bitcast.85), kind=kOutput, calls=%fused_computation.14 | convolution fusion | flops 4294967296 | bytes 17825792 | tf_op jit(solution)/shard_map/dot_general | solution.py:68
  745.3 1.5 fusion.20
  746.8 1.8 copy.34
  748.6 31.2 %all-reduce.6.cloned.1.call-done = f32[1,512,512]{2,1,0:T(8,128)} async-done(((f32[1,512,512]{2,1,0:T(8,128)}), f32[1,512,512]{2,1,0:T(8,128)}) %all-reduce.6.cloned.1.call-update) | async-done | bytes 1048592 | tf_op jit(solution)/shard_map/psum | solution.py:72
  779.8 2.3 copy.59
  (32 shorter events, 2.2 us)
Async XLA Ops:
  7.2 339.5 %reduce-scatter.2.cloned.1.call-start = ((), (), s32[]{:S(2)}) async-start(), calls=%async_computation.1 | async-start | bytes 18874368 | tf_op jit(solution)/shard_map/reduce_scatter | solution.py:60
  64.0 418.4 %all-reduce.4.cloned.1.call-start = ((), (), s32[]{:S(2)}) async-start(), calls=%async_computation.2 | async-start | bytes 2097152 | tf_op jit(solution)/shard_map/psum | solution.py:63
  353.4 373.8 %all-gather.2.cloned.1.call-start = ((), (), s32[]{:S(2)}) async-start(), calls=%async_computation.3 | async-start | bytes 9437184 | tf_op jit(solution)/shard_map/all_gather | solution.py:67
  510.4 80.6 %copy-start = (f32[64,16,512]{2,1,0:T(8,128)S(1)}, f32[64,16,512]{2,1,0:T(8,128)}, u32[]{:S(2)}) copy-start(f32[64,16,512]{2,1,0:T(8,128)} %reduce-scatter.2.cloned.1.call-done) | copy-start | bytes 6291460
  592.6 3.9 copy-start.3
  596.6 3.4 copy-start.1
  600.0 0.8 copy-start.2
  603.1 176.7 %all-reduce.6.cloned.1.call-start = ((), (), s32[]{:S(2)}) async-start(), calls=%async_computation.4 | async-start | bytes 2097152 | tf_op jit(solution)/shard_map/psum | solution.py:72
Sparse Core Ops, SparseCore 0:
  64.1 282.4 reduce-scatter.1
  353.5 128.8 all-reduce.3
  603.2 123.8 all-gather.1
  745.4 34.2 all-reduce.5
where the time goes:
time: 796 us; the launch traced here: 789 us
  waiting for transfers between devices  566 us (71%)
  other arithmetic  103 us (13%)
  matrix products  67.8 us (9%)
  blocking collectives  28 us (4%)
  between operations  14.6 us (2%)
  local copies, waits for them, and re-layouts  8.84 us (1%)
    reduce_scatter x1, waiting for transfers between devices, per_device(): share = lax.psum_scatter(local_sum, 'sum', scatter_dimension=0, tiled=True)  282 us
    psum x1, waiting for transfers between devices, per_device(): gram = lax.psum(gram_part, ('sum', 'mode'))  129 us
    all_gather x1, waiting for transfers between devices, per_device(): pieces = lax.all_gather(rounded, 'sum', axis=0, tiled=True)  124 us
    another operation x8, other arithmetic, orthonormal(): ikk = lax.linalg.triangular_solve(lkk, eye, left_side=True, lower=True)  50.5 us
    another operation x12, other arithmetic, orthonormal(): lkk = jnp.linalg.cholesky(diag)  49.8 us
    psum x1, waiting for transfers between devices, per_device(): carries = lax.psum(partial_carry, 'mode')  31.2 us
    psum x1, blocking collectives, per_device(): mapped = lax.psum(partial_map, 'mode').astype(jnp.bfloat16)  28 us
    dot_general x1, matrix products, per_device(): lax.dot_general(pieces, left_cores, (((0, 1), (1, 2)), ((), ())), preferr...  18.2 us
  transfers between devices with their start and end apart: 4, of which 4 were waited for; matrix products, arithmetic and copies ran while one was open for 0% of the time, Pallas kernels for 0%

commit v1 on v0

--- a/solution.py
+++ b/solution.py
@@ -64,7 +64,12 @@
     basis = orthonormal(flat_share, gram)
     block = basis.reshape(share.shape)
     rounded = block.astype(jnp.bfloat16)
-    pieces = lax.all_gather(rounded, "sum", axis=0, tiled=True)
+    ring = [rounded]
+    for hop in range(7):
+        ring.append(lax.ppermute(ring[-1], "sum", [(dev, (dev + 1) % 8) for dev in range(8)]))
+    pieces = jnp.roll(
+        jnp.concatenate(ring[::-1], axis=0), (lax.axis_index("sum") + 1) * ring[0].shape[0], axis=0
+    )
     partial_carry = lax.dot_general(
         pieces, left_cores, (((0, 1), (1, 2)), ((), ())), preferred_element_type=jnp.float32
     )

time: 796 us -> 882 us (1.11)
  local copies, waits for them, and re-layouts: 8.84 us -> 73.1 us
  waiting for transfers between devices: 566 us -> 580 us
  starting transfers between devices: 0.67 us -> 13 us
    ppermute x0 -> x7, waiting for transfers between devices: none -> 146 us  [per_device(): lax.ppermute(ring[-1], 'sum', [(dev, (dev + 1) % 8) for dev in range(8)])]
    all_gather x1 -> x0, waiting for transfers between devices: 124 us -> none  [per_device(): pieces = lax.all_gather(rounded, 'sum', axis=0, tiled=True)]
    concatenate x0 -> x1, local copies, waits for them, and re-layouts: none -> 37.5 us  [per_device(): jnp.roll(jnp.concatenate(ring[::-1], axis=0), (lax.axis_index('sum') + 1)...]
    ppermute x0 -> x7, local copies, waits for them, and re-layouts: none -> 22 us  [per_device(): lax.ppermute(ring[-1], 'sum', [(dev, (dev + 1) % 8) for dev in range(8)])]
    reduce_scatter x1, waiting for transfers between devices: 282 us -> 271 us  [per_device(): share = lax.psum_scatter(local_sum, 'sum', scatter_dimension=0, tiled=True)]
    psum x1, starting transfers between devices: 0.3 us -> 11.2 us  [per_device(): gram = lax.psum(gram_part, ('sum', 'mode'))]
  transfers between devices with their start and end apart: 4 -> 10, of which waited for: 4 -> 10; matrix products, arithmetic and copies ran while one was open for 0% -> 3% of each run, Pallas kernels for 0% -> 0%
where the time goes in v1:
time: 882 us; the launch traced here: 871 us
  waiting for transfers between devices  580 us (66%)
  other arithmetic  94.7 us (11%)
  local copies, waits for them, and re-layouts  73.1 us (8%)
  matrix products  67.3 us (8%)
  blocking collectives  28 us (3%)
  between operations  14.6 us (2%)
  starting transfers between devices  13 us (1%)
    reduce_scatter x1, waiting for transfers between devices, per_device(): share = lax.psum_scatter(local_sum, 'sum', scatter_dimension=0, tiled=True)  271 us
    ppermute x7, waiting for transfers between devices, per_device(): lax.ppermute(ring[-1], 'sum', [(dev, (dev + 1) % 8) for dev in range(8)])  146 us
    psum x1, waiting for transfers between devices, per_device(): gram = lax.psum(gram_part, ('sum', 'mode'))  129 us
    another operation x12, other arithmetic, orthonormal(): lkk = jnp.linalg.cholesky(diag)  49.9 us
    another operation x8, other arithmetic, orthonormal(): ikk = lax.linalg.triangular_solve(lkk, eye, left_side=True, lower=True)  42.3 us
    concatenate x1, local copies, waits for them, and re-layouts, per_device(): jnp.roll(jnp.concatenate(ring[::-1], axis=0), (lax.axis_index('sum') + 1)...  37.5 us
    psum x1, waiting for transfers between devices, per_device(): carries = lax.psum(partial_carry, 'mode')  33.2 us
    psum x1, blocking collectives, per_device(): mapped = lax.psum(partial_map, 'mode').astype(jnp.bfloat16)  28 us
  transfers between devices with their start and end apart: 10, of which 10 were waited for; matrix products, arithmetic and copies ran while one was open for 3% of the time, Pallas kernels for 0%

profile of v1, /device:TPU:0, one launch (start us, length us, event | category | flops | bytes accessed | tf_op | source)
XLA Modules:
  0.0 870.6 jit_solution(498127510226466390)
XLA Ops:
  7.2 17.1 %fusion.16 = f32[1,512,512]{2,1,0:T(8,128)S(1)} fusion(bf16[16,512,512]{2,1,0:T(8,128)(2,1)} %param.8, bf16[512,16,512]{2,1,0:T(8,128)(2,1)} %bitcast.84), kind=kOutput, calls=%fused_computation.15 | convolution fusion | flops 4294967296 | bytes 17825792 | tf_op jit(solution)/shard_map/dot_general | solution.py:51
  24.3 28.0 %all-reduce.7 = bf16[1,512,512]{2,1,0:T(8,128)(2,1)S(1)} all-reduce(f32[1,512,512]{2,1,0:T(8,128)S(1)} %fusion.16), channel_id=1, replica_groups=mesh['sum'=8,'mode'=4] {'mode'}, use_global_device_ids=true, to_apply=%region_0.0 | all-reduce | flops 262144 | bytes 1572864 | tf_op jit(solution)/shard_map/psum | solution.py:54
  52.3 11.6 %convolution_bitcast_fusion = f32[512,16,512]{2,1,0:T(8,128)} fusion(bf16[1,512,512]{2,1,0:T(8,128)(2,1)S(1)} %all-reduce.7, bf16[1,512,16,512]{3,2,1,0:T(8,128)(2,1)} %param.6), kind=kOutput, calls=%fused_computation | convolution fusion | flops 4294967296 | bytes 25690112 | tf_op jit(solution)/shard_map/dot_general | solution.py:55
  64.0 11.2 %all-reduce.4.cloned.1.call-start = ((), (), s32[]{:S(2)}) async-start(), calls=%async_computation.2 | async-start | bytes 2097152 | tf_op jit(solution)/shard_map/psum | solution.py:63
  75.2 271.3 %reduce-scatter.2.cloned.1.call-done = f32[64,16,512]{2,1,0:T(8,128)} async-done(((f32[512,16,512]{2,1,0:T(8,128)}), f32[64,16,512]{2,1,0:T(8,128)}) %reduce-scatter.2.cloned.1.call-update) | async-done | bytes 2097168 | tf_op jit(solution)/shard_map/reduce_scatter | solution.py:60
  346.5 6.7 convolution_bitcast_fusion.1
  353.3 129.0 %all-reduce.4.cloned.1.call-done = f32[512,512]{0,1:T(8,128)} async-done(((f32[512,512]{0,1:T(8,128)}), f32[512,512]{0,1:T(8,128)}) %all-reduce.4.cloned.1.call-update) | async-done | bytes 1048592 | tf_op jit(solution)/shard_map/psum | solution.py:63
  482.4 0.8 slice.79
  483.3 0.9 fusion.65
  484.2 11.7 %cholesky.74 = f32[128,128]{1,0:T(8,128)S(1)} custom-call(f32[128,128]{1,0:T(8,128)S(1)} %fusion.65), custom_call_target="Cholesky" | custom-call | tf_op jit(solution)/shard_map/jit(cholesky)/cholesky | solution.py:28
  497.2 9.8 %custom-call.8 = f32[1,128,128]{1,2,0:T(8,128)S(1)} custom-call(f32[1,128,128]{2,1,0:T(8,128)S(1)} %fusion.51), custom_call_target="InvertDiagBlocksLowerTriangular" | custom-call | tf_op jit(solution)/shard_map/triangular_solve/custom-call.0 | solution.py:29
  507.3 1.2 fusion.31
  508.6 1.7 convolution_subtract_fusion
  510.5 11.7 %cholesky.85 = f32[128,128]{1,0:T(8,128)S(1)} custom-call(f32[128,128]{1,0:T(8,128)S(1)} %fusion.63), custom_call_target="Cholesky" | custom-call | tf_op jit(solution)/shard_map/jit(cholesky)/cholesky | solution.py:28
  523.5 10.2 %custom-call.9 = f32[1,128,128]{1,2,0:T(8,128)S(1)} custom-call(f32[1,128,128]{2,1,0:T(8,128)S(1)} %fusion.52), custom_call_target="InvertDiagBlocksLowerTriangular" | custom-call | tf_op jit(solution)/shard_map/triangular_solve/custom-call.0 | solution.py:29
  535.5 11.7 %cholesky.96 = f32[128,128]{1,0:T(8,128)S(1)} custom-call(f32[128,128]{1,0:T(8,128)S(1)} %fusion.61), custom_call_target="Cholesky" | custom-call | tf_op jit(solution)/shard_map/jit(cholesky)/cholesky | solution.py:28
  548.7 9.8 %custom-call.10 = f32[1,128,128]{1,2,0:T(8,128)S(1)} custom-call(f32[1,128,128]{2,1,0:T(8,128)S(1)} %fusion.53), custom_call_target="InvertDiagBlocksLowerTriangular" | custom-call | tf_op jit(solution)/shard_map/triangular_solve/custom-call.0 | solution.py:29
  559.4 11.9 %cholesky.107 = f32[128,128]{1,0:T(8,128)S(1)} custom-call(f32[128,128]{1,0:T(8,128)S(1)} %fusion.59), custom_call_target="Cholesky" | custom-call | tf_op jit(solution)/shard_map/jit(cholesky)/cholesky | solution.py:28
  572.7 9.8 %custom-call.11 = f32[1,128,128]{1,2,0:T(8,128)S(1)} custom-call(f32[1,128,128]{2,1,0:T(8,128)S(1)} %fusion.54), custom_call_target="InvertDiagBlocksLowerTriangular" | custom-call | tf_op jit(solution)/shard_map/triangular_solve/custom-call.0 | solution.py:29
  583.4 1.0 convolution_subtract_fusion.2
  585.1 2.7 convolution_subtract_fusion.1
  588.4 2.8 fusion.19
  591.8 0.8 copy-done.2
  593.4 1.5 collective-permute-start
  594.9 25.3 %collective-permute-done = bf16[64,16,512]{2,1,0:T(8,128)(2,1)S(1)} collective-permute-done((bf16[64,16,512]{2,1,0:T(8,128)(2,1)S(1)}, bf16[64,16,512]{2,1,0:T(8,128)(2,1)S(1)}, u32[]{:S(2)}, u32[]{:S(2)}) %collective-permute-start) | collective-permute-done | bytes 1048608 | tf_op jit(solution)/shard_map/ppermute | solution.py:69
  620.2 25.8 %collective-permute-done.1 = bf16[64,16,512]{2,1,0:T(8,128)(2,1)S(1)} collective-permute-done((bf16[64,16,512]{2,1,0:T(8,128)(2,1)S(1)}, bf16[64,16,512]{2,1,0:T(8,128)(2,1)S(1)}, u32[]{:S(2)}, u32[]{:S(2)}) %collective-permute-start.1) | collective-permute-done | bytes 1048608 | tf_op jit(solution)/shard_map/ppermute | solution.py:69
  646.0 1.0 copy-done.5
  647.0 24.9 %collective-permute-done.2 = bf16[64,16,512]{2,1,0:T(8,128)(2,1)S(1)} collective-permute-done((bf16[64,16,512]{2,1,0:T(8,128)(2,1)S(1)}, bf16[64,16,512]{2,1,0:T(8,128)(2,1)S(1)}, u32[]{:S(2)}, u32[]{:S(2)}) %collective-permute-start.2) | collective-permute-done | bytes 1048608 | tf_op jit(solution)/shard_map/ppermute | solution.py:69
  671.9 1.0 copy-done.6
  672.9 24.0 %collective-permute-done.3 = bf16[64,16,512]{2,1,0:T(8,128)(2,1)S(1)} collective-permute-done((bf16[64,16,512]{2,1,0:T(8,128)(2,1)S(1)}, bf16[64,16,512]{2,1,0:T(8,128)(2,1)S(1)}, u32[]{:S(2)}, u32[]{:S(2)}) %collective-permute-start.3) | collective-permute-done | bytes 1048608 | tf_op jit(solution)/shard_map/ppermute | solution.py:69
  696.9 1.0 copy-done.7
  697.8 23.0 %collective-permute-done.4 = bf16[64,16,512]{2,1,0:T(8,128)(2,1)S(1)} collective-permute-done((bf16[64,16,512]{2,1,0:T(8,128)(2,1)S(1)}, bf16[64,16,512]{2,1,0:T(8,128)(2,1)S(1)}, u32[]{:S(2)}, u32[]{:S(2)}) %collective-permute-start.4) | collective-permute-done | bytes 1048608 | tf_op jit(solution)/shard_map/ppermute | solution.py:69
  720.9 1.0 copy-done.8
  721.8 22.9 %collective-permute-done.5 = bf16[64,16,512]{2,1,0:T(8,128)(2,1)} collective-permute-done((bf16[64,16,512]{2,1,0:T(8,128)(2,1)S(1)}, bf16[64,16,512]{2,1,0:T(8,128)(2,1)}, u32[]{:S(2)}, u32[]{:S(2)}) %collective-permute-start.5) | collective-permute-done | bytes 1048608 | tf_op jit(solution)/shard_map/ppermute | solution.py:69
  745.0 2.4 copy.60
  747.4 3.2 copy.59
  750.6 3.1 copy.58
  753.7 3.2 copy.57
  756.9 3.1 copy.56
  760.0 3.1 copy.55
  763.1 3.1 copy.54
  766.5 3.1 copy.53
  769.7 37.5 %concatenate.26 = bf16[1024,16,512]{0,2,1:T(8,128)(2,1)} concatenate(bf16[64,16,512]{0,2,1:T(8,128)(2,1)} %copy.53, bf16[64,16,512]{0,2,1:T(8,128)(2,1)} %copy.54, bf16[64,16,512]{0,2,1:T(8,128)(2,1)} %copy.55, bf16[64,16,512]{0,2,1:T(8,128)(2,1)} %copy.56, bf16[64,16,512]{0,2,1:T(8,128)(2,1)} %copy.57, bf16[64,16,512]{0,2,1:T(8,128)(2,1)} %copy.58, bf16[64,16,512]{0,2,1:T(8,128)(2,1)} %copy.59, ...), dimensions={0} | concatenate | bytes 33554432 | tf_op jit(solution)/shard_map/jit(_roll_dynamic)/concatenate | solution.py:70
  807.2 17.7 %fusion.11 = f32[1,512,512]{2,1,0:T(8,128)} fusion(bf16[512,16,512]{2,1,0:T(8,128)(2,1)} %bitcast.85, bf16[1024,16,512]{0,2,1:T(8,128)(2,1)} %concatenate.26, s32[]{:T(128)S(6)} %select_n.17), kind=kOutput, calls=%fused_computation.13 | convolution fusion | flops 4294967296 | bytes 17825796 | tf_op jit(solution)/shard_map/dot_general | solution.py:73
  824.9 1.5 fusion.23
  826.3 1.8 copy.51
  828.1 33.2 %all-reduce.6.cloned.1.call-done = f32[1,512,512]{2,1,0:T(8,128)} async-done(((f32[1,512,512]{2,1,0:T(8,128)}), f32[1,512,512]{2,1,0:T(8,128)}) %all-reduce.6.cloned.1.call-update) | async-done | bytes 1048592 | tf_op jit(solution)/shard_map/psum | solution.py:77
  861.4 2.3 copy.87
  (63 shorter events, 12.8 us)
Async XLA Ops:
  7.2 339.4 %reduce-scatter.2.cloned.1.call-start = ((), (), s32[]{:S(2)}) async-start(), calls=%async_computation.1 | async-start | bytes 18874368 | tf_op jit(solution)/shard_map/reduce_scatter | solution.py:60
  64.0 418.4 %all-reduce.4.cloned.1.call-start = ((), (), s32[]{:S(2)}) async-start(), calls=%async_computation.2 | async-start | bytes 2097152 | tf_op jit(solution)/shard_map/psum | solution.py:63
  353.3 508.1 %all-reduce.6.cloned.1.call-start = ((), (), s32[]{:S(2)}) async-start(), calls=%async_computation.3 | async-start | bytes 2097152 | tf_op jit(solution)/shard_map/psum | solution.py:77
  510.3 72.5 %copy-start = (f32[64,16,512]{2,1,0:T(8,128)S(1)}, f32[64,16,512]{2,1,0:T(8,128)}, u32[]{:S(2)}) copy-start(f32[64,16,512]{2,1,0:T(8,128)} %reduce-scatter.2.cloned.1.call-done) | copy-start | bytes 6291460
  584.4 3.9 copy-start.9
  588.4 3.4 copy-start.1
  591.8 0.9 copy-start.2
  593.4 151.6 %copy-start.3 = (bf16[1024,512]{1,0:T(8,128)(2,1)}, bf16[1024,512]{1,0:T(8,128)(2,1)S(1)}, u32[]{:S(2)}) copy-start(bf16[1024,512]{1,0:T(8,128)(2,1)S(1)} %copy.52) | copy-start | bytes 3145732
  593.4 26.8 %collective-permute-start = (bf16[64,16,512]{2,1,0:T(8,128)(2,1)S(1)}, bf16[64,16,512]{2,1,0:T(8,128)(2,1)S(1)}, u32[]{:S(2)}, u32[]{:S(2)}) collective-permute-start(bf16[64,16,512]{2,1,0:T(8,128)(2,1)S(1)} %bitcast.81), channel_id=1, source_target_pairs={{0,4},{4,8},{8,12},{12,16},{16,20},{20,24},{24,28},{28,0},{1,5},{5... | collective-permute-start | bytes 3145736 | tf_op jit(solution)/shard_map/ppermute | solution.py:69
  620.2 124.8 %copy-start.4 = (bf16[64,16,512]{2,1,0:T(8,128)(2,1)}, bf16[64,16,512]{2,1,0:T(8,128)(2,1)S(1)}, u32[]{:S(2)}) copy-start(bf16[64,16,512]{2,1,0:T(8,128)(2,1)S(1)} %collective-permute-done) | copy-start | bytes 3145732
  620.2 25.8 %collective-permute-start.1 = (bf16[64,16,512]{2,1,0:T(8,128)(2,1)S(1)}, bf16[64,16,512]{2,1,0:T(8,128)(2,1)S(1)}, u32[]{:S(2)}, u32[]{:S(2)}) collective-permute-start(bf16[64,16,512]{2,1,0:T(8,128)(2,1)S(1)} %collective-permute-done), channel_id=1, source_target_pairs={{0,4},{4,8},{8,12},{12,16},{16,20},{20,24},{24,28},{28,0},{1,5},{5... | collective-permute-start | bytes 3145736 | tf_op jit(solution)/shard_map/ppermute | solution.py:69
  646.0 1.0 copy-start.5
  647.0 24.9 %collective-permute-start.2 = (bf16[64,16,512]{2,1,0:T(8,128)(2,1)S(1)}, bf16[64,16,512]{2,1,0:T(8,128)(2,1)S(1)}, u32[]{:S(2)}, u32[]{:S(2)}) collective-permute-start(bf16[64,16,512]{2,1,0:T(8,128)(2,1)S(1)} %collective-permute-done.1), channel_id=1, source_target_pairs={{0,4},{4,8},{8,12},{12,16},{16,20},{20,24},{24,28},{28,0},{1,5},{5... | collective-permute-start | bytes 3145736 | tf_op jit(solution)/shard_map/ppermute | solution.py:69
  671.9 1.0 copy-start.6
  672.9 24.0 %collective-permute-start.3 = (bf16[64,16,512]{2,1,0:T(8,128)(2,1)S(1)}, bf16[64,16,512]{2,1,0:T(8,128)(2,1)S(1)}, u32[]{:S(2)}, u32[]{:S(2)}) collective-permute-start(bf16[64,16,512]{2,1,0:T(8,128)(2,1)S(1)} %collective-permute-done.2), channel_id=1, source_target_pairs={{0,4},{4,8},{8,12},{12,16},{16,20},{20,24},{24,28},{28,0},{1,5},{5... | collective-permute-start | bytes 3145736 | tf_op jit(solution)/shard_map/ppermute | solution.py:69
  696.9 1.0 copy-start.7
  697.8 23.0 %collective-permute-start.4 = (bf16[64,16,512]{2,1,0:T(8,128)(2,1)S(1)}, bf16[64,16,512]{2,1,0:T(8,128)(2,1)S(1)}, u32[]{:S(2)}, u32[]{:S(2)}) collective-permute-start(bf16[64,16,512]{2,1,0:T(8,128)(2,1)S(1)} %collective-permute-done.3), channel_id=1, source_target_pairs={{0,4},{4,8},{8,12},{12,16},{16,20},{20,24},{24,28},{28,0},{1,5},{5... | collective-permute-start | bytes 3145736 | tf_op jit(solution)/shard_map/ppermute | solution.py:69
  720.9 1.0 copy-start.8
  721.8 22.9 %collective-permute-start.5 = (bf16[64,16,512]{2,1,0:T(8,128)(2,1)S(1)}, bf16[64,16,512]{2,1,0:T(8,128)(2,1)}, u32[]{:S(2)}, u32[]{:S(2)}) collective-permute-start(bf16[64,16,512]{2,1,0:T(8,128)(2,1)S(1)} %collective-permute-done.4), channel_id=1, source_target_pairs={{0,4},{4,8},{8,12},{12,16},{16,20},{20,24},{24,28},{28,0},{1,5},{5... | collective-permute-start | bytes 3145736 | tf_op jit(solution)/shard_map/ppermute | solution.py:69
  744.8 21.8 %collective-permute-start.6 = (bf16[64,16,512]{2,1,0:T(8,128)(2,1)}, bf16[64,16,512]{2,1,0:T(8,128)(2,1)}, u32[]{:S(2)}, u32[]{:S(2)}) collective-permute-start(bf16[64,16,512]{2,1,0:T(8,128)(2,1)} %collective-permute-done.5), channel_id=1, source_target_pairs={{0,4},{4,8},{8,12},{12,16},{16,20},{20,24},{24,28},{28,0},{1,5},{5... | collective-permute-start | bytes 3145736 | tf_op jit(solution)/shard_map/ppermute | solution.py:69
Sparse Core Ops, SparseCore 0:
  64.1 282.3 reduce-scatter.1
  353.4 128.9 all-reduce.3
  825.0 36.3 all-reduce.5
